TPU v7x, 256 devices: a whole 4x4x8 slice. The times are simulated.
256 devices in a mesh: expert: 64 (over y, z, core), tensor: 4 (over x).
Axes of the slice: x: 4, y: 4, z: 8, core: 2. Of those that a mesh axis runs over, the one named last changes fastest.
Arguments:
- tokens: bfloat16 [8192, 2048], P('expert', 'tensor'), may hold values from -6 to 6
- labels: int32 [8192, 1], P('expert'), may hold values from 0 to 31, as said below
- domain_ids: int32 [8192], P('expert'), may hold values from 0 to 21
- domain_weights: float32 [22], replicated, may hold values from 0.02 to 0.5
- cotangent: bfloat16 [8192, 2048], P('expert', 'tensor'), may hold values from -6 to 6
- gate_weight: bfloat16 [64, 2048, 2048], P('expert', None, 'tensor'), may hold values from -0.125 to 0.125
- up_weight: bfloat16 [64, 2048, 2048], P('expert', None, 'tensor'), may hold values from -0.125 to 0.125
- down_weight: bfloat16 [64, 2048, 2048], P('expert', 'tensor'), may hold values from -0.09375 to 0.09375
Outputs:
- layer_out: bfloat16 [8192, 2048], P('expert', 'tensor')
- input_grad: bfloat16 [8192, 2048], P('expert', 'tensor')
- gate_grad: bfloat16 [64, 2048, 2048], P('expert', None, 'tensor')
- up_grad: bfloat16 [64, 2048, 2048], P('expert', None, 'tensor')
- down_grad: bfloat16 [64, 2048, 2048], P('expert', 'tensor')
Inputs may be any that keep to these rules, and one draw needn't show every extreme that they name: `labels`: among the rows of one device (aligned blocks of 128 rows) no label appears more than 8 times, and every such block has some label exactly 8 times.
All inputs are finite; a program needn't handle non-finite values.
Results may differ from a plain program's by a relative error of at most 0.0058.
Values may be sent and summed in bfloat16 or wider, within the bound.
No kernel may reach another device: no remote copies, remote signals or barrier semaphores. Data moves between devices by JAX's collectives and lax.ppermute only.
A program may use at most 320 MiB of HBM per device.

v0:
```python
import jax
import jax.numpy as jnp
from jax import lax
from jax.sharding import PartitionSpec as P

SPLIT = 2


def partner(value, axis, stride):
    return lax.ppermute(value, axis, [(i, i ^ 1 << stride) for i in range(lax.axis_size(axis))])


def silu_parts(gate_pre):
    squash = jax.nn.sigmoid(gate_pre)
    return (squash, gate_pre * squash)


def body(
    tokens, labels, domain_ids, domain_weights, cotangent, gate_weight, up_weight, down_weight
):
    n_expert = lax.axis_size("expert")
    tok_rows = tokens.shape[0]
    experts_all = n_expert // SPLIT
    capacity = 2 * tok_rows // experts_all
    half_cap = capacity // 2
    parity = lax.axis_index("expert") % 2
    lang_label = labels[:, 0]
    dom_hot = (
        domain_ids[:, None] == jnp.arange(domain_weights.shape[0], dtype=jnp.int32)[None, :]
    ).astype(jnp.float32)
    tok_scale = jnp.sum(dom_hot * domain_weights[None, :], axis=1)
    grad_rows = (tok_scale[:, None] * cotangent.astype(jnp.float32)).astype(jnp.bfloat16)
    lab_hot = (lang_label[:, None] == jnp.arange(experts_all, dtype=jnp.int32)[None, :]).astype(
        jnp.float32
    )
    row_ids = jnp.arange(tok_rows, dtype=jnp.int32)
    earlier = (row_ids[None, :] < row_ids[:, None]).astype(jnp.float32)
    before = jnp.dot(earlier, lab_hot, precision=lax.Precision.HIGHEST)
    slot_pos = jnp.sum(before * lab_hot, axis=1).astype(jnp.int32)
    target_row = lang_label * capacity + slot_pos
    sources = jnp.stack((tokens, grad_rows))
    sources = lax.all_gather(sources, "tensor", axis=2, tiled=True)
    slot_ids = jnp.arange(n_expert * capacity, dtype=jnp.int32)
    dispatch_map = (slot_ids[:, None] // capacity // SPLIT == lang_label[None, :]) & (
        slot_ids[:, None] % capacity == slot_pos[None, :]
    )
    dispatch_map = dispatch_map.astype(jnp.bfloat16)
    outbound = jnp.einsum(
        "rt,ktw->krw", dispatch_map, sources, preferred_element_type=jnp.float32
    ).astype(jnp.bfloat16)
    outbound = outbound.reshape(2, n_expert, capacity, sources.shape[2])
    arrived = lax.all_to_all(outbound, "expert", split_axis=1, concat_axis=1, tiled=True)
    rows_all = n_expert * capacity
    feat_width = arrived.shape[3]
    routed = arrived[0].reshape(rows_all, feat_width)
    routed_grad = arrived[1].reshape(rows_all, feat_width)
    w_gate = gate_weight[0]
    w_up = up_weight[0]
    w_down = down_weight[0]
    contract_rows = (((0,), (0,)), ((), ()))
    contract_cols = (((1,), (1,)), ((), ()))
    gate_pre = jnp.dot(routed, w_gate, preferred_element_type=jnp.float32)
    up_pre = jnp.dot(routed, w_up, preferred_element_type=jnp.float32)
    squash, activated = silu_parts(gate_pre)
    hidden = (activated * up_pre).astype(jnp.bfloat16)
    out_part = jnp.dot(hidden, w_down, preferred_element_type=jnp.float32)
    grad_hidden = lax.dot_general(
        routed_grad, w_down, contract_cols, preferred_element_type=jnp.float32
    )
    grad_gate_pre = (grad_hidden * up_pre * squash * (1.0 + gate_pre * (1.0 - squash))).astype(
        jnp.bfloat16
    )
    grad_up_pre = (grad_hidden * activated).astype(jnp.bfloat16)
    gate_grad = lax.dot_general(
        routed, grad_gate_pre, contract_rows, preferred_element_type=jnp.float32
    ).astype(jnp.bfloat16)[None]
    up_grad = lax.dot_general(
        routed, grad_up_pre, contract_rows, preferred_element_type=jnp.float32
    ).astype(jnp.bfloat16)[None]
    down_grad = lax.dot_general(
        hidden, routed_grad, contract_rows, preferred_element_type=jnp.float32
    ).astype(jnp.bfloat16)[None]
    input_part = lax.dot_general(
        grad_gate_pre, w_gate, contract_cols, preferred_element_type=jnp.float32
    ) + lax.dot_general(grad_up_pre, w_up, contract_cols, preferred_element_type=jnp.float32)
    out_part = out_part.reshape(n_expert, capacity, feat_width)
    input_part = input_part.reshape(n_expert, capacity, feat_width)
    out_share, input_share = (
        lax.psum_scatter(out_part, "tensor", scatter_dimension=2, tiled=True),
        lax.psum_scatter(input_part, "tensor", scatter_dimension=2, tiled=True),
    )
    partial_value = jnp.stack((out_share, input_share))
    kept = jnp.where(parity == 0, partial_value[:, :, :half_cap], partial_value[:, :, half_cap:])
    handed = jnp.where(parity == 0, partial_value[:, :, half_cap:], partial_value[:, :, :half_cap])
    summed = kept + partner(handed, "expert", 0)
    going_back = summed.astype(jnp.bfloat16)
    returned = lax.all_to_all(going_back, "expert", split_axis=1, concat_axis=1, tiled=True)
    home_ids = jnp.arange(n_expert * half_cap, dtype=jnp.int32)
    home_map = (home_ids[:, None] == target_row[None, :]).astype(jnp.bfloat16)
    flat_back = returned.reshape(2, n_expert * half_cap, returned.shape[3])
    gathered_home = jnp.einsum(
        "rt,krw->ktw", home_map, flat_back, preferred_element_type=jnp.float32
    ).astype(jnp.bfloat16)
    return (gathered_home[0], gathered_home[1], gate_grad, up_grad, down_grad)


def solution(mesh):
    return jax.shard_map(
        body,
        mesh=mesh,
        in_specs=(
            P("expert", "tensor"),
            P("expert", None),
            P("expert"),
            P(),
            P("expert", "tensor"),
            P("expert", None, "tensor"),
            P("expert", None, "tensor"),
            P("expert", "tensor", None),
        ),
        out_specs=(
            P("expert", "tensor"),
            P("expert", "tensor"),
            P("expert", None, "tensor"),
            P("expert", None, "tensor"),
            P("expert", "tensor", None),
        ),
        check_vma=False,
    )
```

profile of v0, /device:TPU:1, one launch (start us, length us, event | category | flops | bytes accessed | tf_op | source)
XLA Modules:
  0.0 302.7 jit_solution(17173675187760145169)
XLA Ops:
  7.2 0.0 copy-start
  7.2 0.0 all-gather.2.cloned.1.call-start
  7.2 0.9 select_reduce_fusion
  8.1 1.0 fusion.24
  9.1 1.6 pad_maximum_fusion.1
  10.8 0.0 all-gather.2.cloned.1.call-update
  10.8 0.0 reduce-scatter.5.cloned.1.call-start
  10.8 0.9 fusion.15
  11.7 28.7 %all-gather.2.cloned.1.call-done = bf16[2,128,2048]{2,1,0:T(8,128)(2,1)} async-done(((bf16[2,128,512]{2,1,0:T(8,128)(2,1)}), bf16[2,128,2048]{2,1,0:T(8,128)(2,1)}) %all-gather.2.cloned.1.call-update) | async-done | bytes 1048592 | tf_op jit(solution)/shard_map/all_gather | solution.py:42
  40.4 2.5 convert_bitcast_fusion
  42.9 0.6 copy.27
  43.5 0.0 copy-start.6
  43.5 107.7 %all_to_all.10 = bf16[2,64,8,2048]{3,2,0,1:T(8,128)(2,1)S(1)} all-to-all(bf16[2,64,8,2048]{3,2,0,1:T(8,128)(2,1)S(1)} %copy.27), channel_id=1, replica_groups=mesh['expert'=64,'tensor'=4] {'expert'}, dimensions={1} | all-to-all | bytes 8388608 | tf_op jit(solution)/shard_map/all_to_all | solution.py:52
  151.2 0.0 copy-done.6
  151.3 1.2 fusion.12
  152.5 1.9 copy-done.5
  154.4 1.3 fusion.5
  155.6 0.0 copy-done.1
  155.7 1.6 multiply_convert_fusion.2
  157.3 0.0 copy-start.7
  157.3 0.0 copy-start.9
  157.3 1.3 fusion.10
  158.6 0.0 copy-done.7
  158.6 0.0 copy-done.10
  158.7 3.3 %add_bitcast_fusion = f32[64,8,2048]{2,1,0:T(8,128)} fusion(f32[512,2048]{1,0:T(8,128)S(1)} %fusion.10, bf16[512,512]{1,0:T(8,128)(2,1)S(1)} %get-tuple-element.27, bf16[1,2048,512]{2,1,0:T(8,128)(2,1)S(1)} %copy-done), kind=kOutput, calls=%fused_computation | convolution fusion | flops 1074790400 | bytes 11010048 | tf_op jit(solution)/shard_map/dot_general | solution.py:85
  161.9 0.0 reduce-scatter.5.cloned.1.call-update
  161.9 0.0 reduce-scatter.3.cloned.1.call-start
  162.0 4.8 %fusion.3 = f32[64,8,2048]{2,1,0:T(8,128)} fusion(bf16[1,512,2048]{2,1,0:T(8,128)(2,1)} %param.15, bf16[512,512]{1,0:T(8,128)(2,1)S(1)} %get-tuple-element.25), kind=kOutput, calls=%fused_computation.12 | convolution fusion | flops 1073741824 | bytes 6815744 | tf_op jit(solution)/shard_map/dot_general | solution.py:66
  166.8 0.0 reduce-scatter.3.cloned.1.call-update
  166.9 40.1 %reduce-scatter.5.cloned.1.call-done = f32[64,8,512]{2,1,0:T(8,128)} async-done(((f32[64,8,2048]{2,1,0:T(8,128)}), f32[64,8,512]{2,1,0:T(8,128)}) %reduce-scatter.5.cloned.1.call-update) | async-done | bytes 1048592 | tf_op jit(solution)/shard_map/reduce_scatter | solution.py:90
  207.0 51.8 %reduce-scatter.3.cloned.1.call-done = f32[64,8,512]{2,1,0:T(8,128)} async-done(((f32[64,8,2048]{2,1,0:T(8,128)}), f32[64,8,512]{2,1,0:T(8,128)}) %reduce-scatter.3.cloned.1.call-update) | async-done | bytes 1048592 | tf_op jit(solution)/shard_map/reduce_scatter | solution.py:89
  258.8 2.8 broadcast_select_fusion
  261.6 0.0 copy-start.12
  261.7 0.7 collective-permute-start
  262.4 2.3 collective-permute-done
  264.7 0.4 add_convert_fusion
  265.1 1.0 copy.28
  266.1 10.4 %all-to-all-start.1 = ((bf16[2,64,4,512]{3,2,0,1:T(4,128)(2,1)}), bf16[2,64,4,512]{3,2,0,1:T(4,128)(2,1)S(1)}, u32[]{:S(2)}, u32[]{:S(2)}) async-start(bf16[2,64,4,512]{3,2,0,1:T(4,128)(2,1)} %copy.28), calls=%async_computation.3 | async-start | bytes 1048576 | tf_op jit(solution)/shard_map/all_to_all | solution.py:97
  276.5 0.0 copy-start.8
  276.5 4.5 %fusion.2 = bf16[1,512,2048]{2,1,0:T(8,128)(2,1)} fusion(bf16[512,512]{1,0:T(8,128)(2,1)} %copy-done.9, bf16[2,64,8,2048]{3,2,0,1:T(8,128)(2,1)} %copy-done.1), kind=kOutput, calls=%fused_computation.7 | convolution fusion | flops 1074790400 | bytes 4718592 | tf_op jit(solution)/shard_map/dot_general | solution.py:80
  281.0 0.0 copy-done.8
  281.0 2.6 fusion
  283.7 2.6 fusion.1
  286.3 7.5 %all-to-all-done.1 = bf16[2,64,4,512]{3,2,0,1:T(4,128)(2,1)S(1)} async-done(((bf16[2,64,4,512]{3,2,0,1:T(4,128)(2,1)}), bf16[2,64,4,512]{3,2,0,1:T(4,128)(2,1)S(1)}, u32[]{:S(2)}, u32[]{:S(2)}) %all-to-all-start.1) | async-done | bytes 524320 | tf_op jit(solution)/shard_map/all_to_all | solution.py:97
  293.8 0.4 copy.29
  294.2 0.3 fusion.14
  294.6 0.8 copy.31
  295.4 0.8 copy.32
  (18 shorter events, 0.1 us)
Async XLA Ops:
  7.2 148.5 %copy-start = (bf16[1,2048,512]{2,1,0:T(8,128)(2,1)S(1)}, bf16[1,2048,512]{2,1,0:T(8,128)(2,1)}, u32[]{:S(2)}) copy-start(bf16[1,2048,512]{2,1,0:T(8,128)(2,1)} %param.14) | copy-start | bytes 6291460
  7.2 33.2 %all-gather.2.cloned.1.call-start = ((), (), s32[]{:S(2)}) async-start(), calls=%async_computation.4 | async-start | bytes 1310720 | tf_op jit(solution)/shard_map/all_gather | solution.py:42
  10.8 196.2 %reduce-scatter.5.cloned.1.call-start = ((), (), s32[]{:S(2)}) async-start(), calls=%async_computation.6 | async-start | bytes 5242880 | tf_op jit(solution)/shard_map/reduce_scatter | solution.py:90
  43.5 107.7 %copy-start.6 = (bf16[1,2048,512]{2,1,0:T(8,128)(2,1)S(1)}, bf16[1,2048,512]{2,1,0:T(8,128)(2,1)}, u32[]{:S(2)}) copy-start(bf16[1,2048,512]{2,1,0:T(8,128)(2,1)} %param.13) | copy-start | bytes 6291460
  151.2 4.4 %copy-start.1 = (bf16[2,64,8,2048]{3,2,0,1:T(8,128)(2,1)}, bf16[2,64,8,2048]{3,2,0,1:T(8,128)(2,1)S(1)}, u32[]{:S(2)}) copy-start(bf16[2,64,8,2048]{3,2,0,1:T(8,128)(2,1)S(1)} %all_to_all.10) | copy-start | bytes 12582916
  151.2 3.1 %copy-start.5 = (bf16[1,512,2048]{2,1,0:T(8,128)(2,1)S(1)}, bf16[1,512,2048]{2,1,0:T(8,128)(2,1)}, u32[]{:S(2)}) copy-start(bf16[1,512,2048]{2,1,0:T(8,128)(2,1)} %param.15) | copy-start | bytes 6291460
  157.3 1.3 copy-start.7
  157.3 1.3 copy-start.10
  157.3 4.7 %copy-start.9 = (bf16[512,512]{1,0:T(8,128)(2,1)}, bf16[512,512]{1,0:T(8,128)(2,1)S(1)}, u32[]{:S(2)}) copy-start(bf16[512,512]{1,0:T(8,128)(2,1)S(1)} %get-tuple-element.25) | copy-start | bytes 1572868
  161.9 96.9 %reduce-scatter.3.cloned.1.call-start = ((), (), s32[]{:S(2)}) async-start(), calls=%async_computation.5 | async-start | bytes 5242880 | tf_op jit(solution)/shard_map/reduce_scatter | solution.py:89
  207.0 57.7 %copy-start.3 = (f32[64,8,512]{2,1,0:T(8,128)S(1)}, f32[64,8,512]{2,1,0:T(8,128)}, u32[]{:S(2)}) copy-start(f32[64,8,512]{2,1,0:T(8,128)} %reduce-scatter.5.cloned.1.call-done) | copy-start | bytes 3145732
  258.8 5.8 %copy-start.4 = (f32[64,8,512]{2,1,0:T(8,128)S(1)}, f32[64,8,512]{2,1,0:T(8,128)}, u32[]{:S(2)}) copy-start(f32[64,8,512]{2,1,0:T(8,128)} %reduce-scatter.3.cloned.1.call-done) | copy-start | bytes 3145732
  261.6 14.8 %copy-start.12 = (s32[128,1]{0,1:T(1,128)S(1)}, s32[128,1]{0,1:T(1,128)}, u32[]{:S(2)}) copy-start(s32[128,1]{0,1:T(1,128)} %param.9) | copy-start | bytes 1540
  261.7 3.0 collective-permute-start
  266.1 27.7 %all-to-all-start.1 = ((bf16[2,64,4,512]{3,2,0,1:T(4,128)(2,1)}), bf16[2,64,4,512]{3,2,0,1:T(4,128)(2,1)S(1)}, u32[]{:S(2)}, u32[]{:S(2)}) async-start(bf16[2,64,4,512]{3,2,0,1:T(4,128)(2,1)} %copy.28), calls=%async_computation.3 | async-start | bytes 1048576 | tf_op jit(solution)/shard_map/all_to_all | solution.py:97
  276.5 4.5 %copy-start.2 = (bf16[2,64,8,2048]{3,2,0,1:T(8,128)(2,1)S(1)}, bf16[2,64,8,2048]{3,2,0,1:T(8,128)(2,1)}, u32[]{:S(2)}) copy-start(bf16[2,64,8,2048]{3,2,0,1:T(8,128)(2,1)} %copy-done.1) | copy-start | bytes 12582916
  276.5 4.5 %copy-start.8 = (bf16[512,512]{1,0:T(8,128)(2,1)S(1)}, bf16[512,512]{1,0:T(8,128)(2,1)}, u32[]{:S(2)}) copy-start(bf16[512,512]{1,0:T(8,128)(2,1)} %copy-done.7) | copy-start | bytes 1572868
  281.0 2.6 copy-start.11
Sparse Core Ops, SparseCore 0:
  10.9 29.4 all-gather.1
  162.1 44.8 reduce-scatter.4
  209.7 49.0 reduce-scatter.2
where the time goes:
time: 303 us
  waiting for transfers between devices  130 us (43%)
  blocking collectives  108 us (36%)
  matrix products  27 us (9%)
  between operations  14 us (5%)
  starting transfers between devices  11.2 us (4%)
  other arithmetic  6.76 us (2%)
  local copies, waits for them, and re-layouts  5.46 us (2%)
    all_to_all x1, blocking collectives, body(): lax.all_to_all(outbound, 'expert', split_axis=1, concat_axis=1, tiled=True)  108 us
    reduce_scatter x1, waiting for transfers between devices, body(): lax.psum_scatter(out_part, 'tensor', scatter_dimension=2, tiled=True)  51.8 us
    reduce_scatter x1, waiting for transfers between devices, body(): lax.psum_scatter(input_part, 'tensor', scatter_dimension=2, tiled=True)  40.1 us
    all_gather x1, waiting for transfers between devices, body(): sources = lax.all_gather(sources, 'tensor', axis=2, tiled=True)  28.7 us
    all_to_all x1, starting transfers between devices, body(): lax.all_to_all(going_back, 'expert', split_axis=1, concat_axis=1, tiled=T...  10.4 us
    all_to_all x1, waiting for transfers between devices, body(): lax.all_to_all(going_back, 'expert', split_axis=1, concat_axis=1, tiled=T...  7.52 us
  transfers between devices with their start and end apart: 5, of which 5 were waited for; matrix products, arithmetic and copies ran while one was open for 5% of the time, Pallas kernels for 0%

commit v1 on v0

--- a/solution.py
+++ b/solution.py
@@ -39,7 +39,9 @@
     slot_pos = jnp.sum(before * lab_hot, axis=1).astype(jnp.int32)
     target_row = lang_label * capacity + slot_pos
     sources = jnp.stack((tokens, grad_rows))
-    sources = lax.all_gather(sources, "tensor", axis=2, tiled=True)
+    sources = jnp.concatenate(
+        lax.all_to_all(jnp.stack([sources] * lax.axis_size("tensor")), "tensor", 0, 0), axis=2
+    )
     slot_ids = jnp.arange(n_expert * capacity, dtype=jnp.int32)
     dispatch_map = (slot_ids[:, None] // capacity // SPLIT == lang_label[None, :]) & (
         slot_ids[:, None] % capacity == slot_pos[None, :]

time: 303 us -> 293 us (0.967)
  waiting for transfers between devices: 130 us -> 114 us
  starting transfers between devices: 11.2 us -> 16 us
    all_gather x1 -> x0, waiting for transfers between devices: 28.7 us -> none  [body(): sources = lax.all_gather(sources, 'tensor', axis=2, tiled=True)]
    all_to_all x0 -> x1, waiting for transfers between devices: none -> 13.1 us  [body(): lax.all_to_all(jnp.stack([sources] * lax.axis_size('tensor')), 'tensor',...]
    all_to_all x0 -> x1, starting transfers between devices: none -> 4.84 us  [body(): lax.all_to_all(jnp.stack([sources] * lax.axis_size('tensor')), 'tensor',...]
where the time goes in v1:
time: 293 us
  waiting for transfers between devices  114 us (39%)
  blocking collectives  111 us (38%)
  matrix products  25.1 us (9%)
  starting transfers between devices  16 us (5%)
  between operations  14.3 us (5%)
  local copies, waits for them, and re-layouts  6.62 us (2%)
  other arithmetic  6.08 us (2%)
    all_to_all x1, blocking collectives, body(): lax.all_to_all(outbound, 'expert', split_axis=1, concat_axis=1, tiled=True)  111 us
    reduce_scatter x1, waiting for transfers between devices, body(): lax.psum_scatter(out_part, 'tensor', scatter_dimension=2, tiled=True)  51.9 us
    reduce_scatter x1, waiting for transfers between devices, body(): lax.psum_scatter(input_part, 'tensor', scatter_dimension=2, tiled=True)  39.2 us
    all_to_all x1, waiting for transfers between devices, body(): lax.all_to_all(jnp.stack([sources] * lax.axis_size('tensor')), 'tensor',...  13.1 us
    all_to_all x1, starting transfers between devices, body(): lax.all_to_all(going_back, 'expert', split_axis=1, concat_axis=1, tiled=T...  10.4 us
    all_to_all x1, waiting for transfers between devices, body(): lax.all_to_all(going_back, 'expert', split_axis=1, concat_axis=1, tiled=T...  7.53 us
  transfers between devices with their start and end apart: 5, of which 5 were waited for; matrix products, arithmetic and copies ran while one was open for 5% of the time, Pallas kernels for 0%

profile of v1, /device:TPU:1, one launch (start us, length us, event | category | flops | bytes accessed | tf_op | source)
XLA Modules:
  0.0 292.6 jit_solution(17322614337723214446)
XLA Ops:
  7.2 0.0 copy-start
  7.2 0.9 select_reduce_fusion
  8.1 1.0 fusion.24
  9.1 0.9 pad_maximum_fusion.1
  10.0 1.1 stack.28
  11.1 4.8 %all-to-all-start = ((bf16[4,2,128,512]{3,2,1,0:T(8,128)(2,1)}), bf16[4,2,128,512]{3,2,1,0:T(8,128)(2,1)S(1)}, u32[]{:S(2)}, u32[]{:S(2)}) async-start(bf16[4,2,128,512]{3,2,1,0:T(8,128)(2,1)} %stack.28), calls=%async_computation | async-start | bytes 2097152 | tf_op jit(solution)/shard_map/all_to_all | solution.py:43
  15.9 0.0 copy-done.12
  15.9 0.2 fusion.15
  16.1 13.1 %all-to-all-done = bf16[4,2,128,512]{3,2,1,0:T(8,128)(2,1)S(1)} async-done(((bf16[4,2,128,512]{3,2,1,0:T(8,128)(2,1)}), bf16[4,2,128,512]{3,2,1,0:T(8,128)(2,1)S(1)}, u32[]{:S(2)}, u32[]{:S(2)}) %all-to-all-start) | async-done | bytes 1048608 | tf_op jit(solution)/shard_map/all_to_all | solution.py:43
  29.2 0.1 copy.36
  29.3 1.3 convert_bitcast_fusion
  30.6 0.6 copy.30
  31.2 0.0 copy-start.6
  31.2 110.6 %all_to_all.15 = bf16[2,64,8,2048]{3,2,0,1:T(8,128)(2,1)S(1)} all-to-all(bf16[2,64,8,2048]{3,2,0,1:T(8,128)(2,1)S(1)} %copy.30), channel_id=1, replica_groups=mesh['expert'=64,'tensor'=4] {'expert'}, dimensions={1} | all-to-all | bytes 8388608 | tf_op jit(solution)/shard_map/all_to_all | solution.py:54
  141.8 1.2 fusion.12
  143.0 1.9 copy-done.5
  144.9 1.3 fusion.5
  146.2 0.0 copy-done.1
  146.2 0.0 copy-done
  146.2 1.6 multiply_convert_fusion.2
  147.8 0.0 copy-start.7
  147.9 0.0 copy-start.9
  147.9 1.3 fusion.10
  149.2 0.0 copy-done.7
  149.2 0.0 copy-done.10
  149.2 3.3 %add_bitcast_fusion = f32[64,8,2048]{2,1,0:T(8,128)} fusion(f32[512,2048]{1,0:T(8,128)S(1)} %fusion.10, bf16[512,512]{1,0:T(8,128)(2,1)S(1)} %get-tuple-element.27, bf16[1,2048,512]{2,1,0:T(8,128)(2,1)S(1)} %copy-done), kind=kOutput, calls=%fused_computation | convolution fusion | flops 1074790400 | bytes 11010048 | tf_op jit(solution)/shard_map/dot_general | solution.py:87
  152.4 0.0 reduce-scatter.5.cloned.1.call-update
  152.5 0.0 reduce-scatter.3.cloned.1.call-start
  152.5 4.8 %fusion.3 = f32[64,8,2048]{2,1,0:T(8,128)} fusion(bf16[1,512,2048]{2,1,0:T(8,128)(2,1)} %param.15, bf16[512,512]{1,0:T(8,128)(2,1)S(1)} %get-tuple-element.25), kind=kOutput, calls=%fused_computation.12 | convolution fusion | flops 1073741824 | bytes 6815744 | tf_op jit(solution)/shard_map/dot_general | solution.py:68
  157.3 0.0 reduce-scatter.3.cloned.1.call-update
  157.4 39.2 %reduce-scatter.5.cloned.1.call-done = f32[64,8,512]{2,1,0:T(8,128)} async-done(((f32[64,8,2048]{2,1,0:T(8,128)}), f32[64,8,512]{2,1,0:T(8,128)}) %reduce-scatter.5.cloned.1.call-update) | async-done | bytes 1048592 | tf_op jit(solution)/shard_map/reduce_scatter | solution.py:92
  196.6 51.9 %reduce-scatter.3.cloned.1.call-done = f32[64,8,512]{2,1,0:T(8,128)} async-done(((f32[64,8,2048]{2,1,0:T(8,128)}), f32[64,8,512]{2,1,0:T(8,128)}) %reduce-scatter.3.cloned.1.call-update) | async-done | bytes 1048592 | tf_op jit(solution)/shard_map/reduce_scatter | solution.py:91
  248.5 2.8 broadcast_select_fusion
  251.3 0.7 collective-permute-start
  252.0 2.3 collective-permute-done
  254.3 0.0 copy-done.4
  254.3 0.4 add_convert_fusion
  254.7 1.0 copy.31
  255.7 10.4 %all-to-all-start.2 = ((bf16[2,64,4,512]{3,2,0,1:T(4,128)(2,1)}), bf16[2,64,4,512]{3,2,0,1:T(4,128)(2,1)S(1)}, u32[]{:S(2)}, u32[]{:S(2)}) async-start(bf16[2,64,4,512]{3,2,0,1:T(4,128)(2,1)} %copy.31), calls=%async_computation.4 | async-start | bytes 1048576 | tf_op jit(solution)/shard_map/all_to_all | solution.py:99
  266.1 0.0 copy-start.8
  266.1 4.5 %fusion.2 = bf16[1,512,2048]{2,1,0:T(8,128)(2,1)} fusion(bf16[512,512]{1,0:T(8,128)(2,1)} %copy-done.9, bf16[2,64,8,2048]{3,2,0,1:T(8,128)(2,1)} %copy-done.1), kind=kOutput, calls=%fused_computation.7 | convolution fusion | flops 1074790400 | bytes 4718592 | tf_op jit(solution)/shard_map/dot_general | solution.py:82
  270.6 2.6 fusion
  273.2 2.6 fusion.1
  275.9 7.5 %all-to-all-done.2 = bf16[2,64,4,512]{3,2,0,1:T(4,128)(2,1)S(1)} async-done(((bf16[2,64,4,512]{3,2,0,1:T(4,128)(2,1)}), bf16[2,64,4,512]{3,2,0,1:T(4,128)(2,1)S(1)}, u32[]{:S(2)}, u32[]{:S(2)}) %all-to-all-start.2) | async-done | bytes 524320 | tf_op jit(solution)/shard_map/all_to_all | solution.py:99
  283.4 0.4 copy.32
  283.8 0.4 fusion.14
  284.2 0.8 copy.34
  285.0 0.8 copy.35
  (19 shorter events, 0.1 us)
Async XLA Ops:
  7.2 139.0 %copy-start = (bf16[1,2048,512]{2,1,0:T(8,128)(2,1)S(1)}, bf16[1,2048,512]{2,1,0:T(8,128)(2,1)}, u32[]{:S(2)}) copy-start(bf16[1,2048,512]{2,1,0:T(8,128)(2,1)} %param.14) | copy-start | bytes 6291460
  8.1 7.9 %copy-start.12 = (s32[128,1]{0,1:T(1,128)S(1)}, s32[128,1]{0,1:T(1,128)}, u32[]{:S(2)}) copy-start(s32[128,1]{0,1:T(1,128)} %param.9) | copy-start | bytes 1540
  11.1 18.1 %all-to-all-start = ((bf16[4,2,128,512]{3,2,1,0:T(8,128)(2,1)}), bf16[4,2,128,512]{3,2,1,0:T(8,128)(2,1)S(1)}, u32[]{:S(2)}, u32[]{:S(2)}) async-start(bf16[4,2,128,512]{3,2,1,0:T(8,128)(2,1)} %stack.28), calls=%async_computation | async-start | bytes 2097152 | tf_op jit(solution)/shard_map/all_to_all | solution.py:43
  15.9 180.7 %reduce-scatter.5.cloned.1.call-start = ((), (), s32[]{:S(2)}) async-start(), calls=%async_computation.6 | async-start | bytes 5242880 | tf_op jit(solution)/shard_map/reduce_scatter | solution.py:92
  31.2 110.6 %copy-start.6 = (bf16[1,2048,512]{2,1,0:T(8,128)(2,1)S(1)}, bf16[1,2048,512]{2,1,0:T(8,128)(2,1)}, u32[]{:S(2)}) copy-start(bf16[1,2048,512]{2,1,0:T(8,128)(2,1)} %param.13) | copy-start | bytes 6291460
  141.8 4.4 %copy-start.1 = (bf16[2,64,8,2048]{3,2,0,1:T(8,128)(2,1)}, bf16[2,64,8,2048]{3,2,0,1:T(8,128)(2,1)S(1)}, u32[]{:S(2)}) copy-start(bf16[2,64,8,2048]{3,2,0,1:T(8,128)(2,1)S(1)} %all_to_all.15) | copy-start | bytes 12582916
  141.8 3.1 %copy-start.5 = (bf16[1,512,2048]{2,1,0:T(8,128)(2,1)S(1)}, bf16[1,512,2048]{2,1,0:T(8,128)(2,1)}, u32[]{:S(2)}) copy-start(bf16[1,512,2048]{2,1,0:T(8,128)(2,1)} %param.15) | copy-start | bytes 6291460
  147.8 1.3 copy-start.7
  147.9 1.3 copy-start.10
  147.9 4.7 %copy-start.9 = (bf16[512,512]{1,0:T(8,128)(2,1)}, bf16[512,512]{1,0:T(8,128)(2,1)S(1)}, u32[]{:S(2)}) copy-start(bf16[512,512]{1,0:T(8,128)(2,1)S(1)} %get-tuple-element.25) | copy-start | bytes 1572868
  152.5 96.0 %reduce-scatter.3.cloned.1.call-start = ((), (), s32[]{:S(2)}) async-start(), calls=%async_computation.5 | async-start | bytes 5242880 | tf_op jit(solution)/shard_map/reduce_scatter | solution.py:91
  196.6 57.7 %copy-start.3 = (f32[64,8,512]{2,1,0:T(8,128)S(1)}, f32[64,8,512]{2,1,0:T(8,128)}, u32[]{:S(2)}) copy-start(f32[64,8,512]{2,1,0:T(8,128)} %reduce-scatter.5.cloned.1.call-done) | copy-start | bytes 3145732
  248.5 5.8 %copy-start.4 = (f32[64,8,512]{2,1,0:T(8,128)S(1)}, f32[64,8,512]{2,1,0:T(8,128)}, u32[]{:S(2)}) copy-start(f32[64,8,512]{2,1,0:T(8,128)} %reduce-scatter.3.cloned.1.call-done) | copy-start | bytes 3145732
  251.3 3.0 %collective-permute-start = (f32[2,64,4,512]{3,2,1,0:T(4,128)S(1)}, f32[2,64,4,512]{3,2,1,0:T(4,128)S(1)}, u32[]{:S(2)}, u32[]{:S(2)}) collective-permute-start(f32[2,64,4,512]{3,2,1,0:T(4,128)S(1)} %broadcast_select_fusion), channel_id=1, source_target_pairs={{0,4},{4,0},{8,12},{12,8},{16,20},{20,16},{24,28},{28,24},{32,36},... | collective-permute-start | bytes 3145736 | tf_op jit(solution)/shard_map/ppermute | solution.py:10
  255.7 27.7 %all-to-all-start.2 = ((bf16[2,64,4,512]{3,2,0,1:T(4,128)(2,1)}), bf16[2,64,4,512]{3,2,0,1:T(4,128)(2,1)S(1)}, u32[]{:S(2)}, u32[]{:S(2)}) async-start(bf16[2,64,4,512]{3,2,0,1:T(4,128)(2,1)} %copy.31), calls=%async_computation.4 | async-start | bytes 1048576 | tf_op jit(solution)/shard_map/all_to_all | solution.py:99
  266.1 4.5 %copy-start.2 = (bf16[2,64,8,2048]{3,2,0,1:T(8,128)(2,1)S(1)}, bf16[2,64,8,2048]{3,2,0,1:T(8,128)(2,1)}, u32[]{:S(2)}) copy-start(bf16[2,64,8,2048]{3,2,0,1:T(8,128)(2,1)} %copy-done.1) | copy-start | bytes 12582916
  266.1 4.5 %copy-start.8 = (bf16[512,512]{1,0:T(8,128)(2,1)S(1)}, bf16[512,512]{1,0:T(8,128)(2,1)}, u32[]{:S(2)}) copy-start(bf16[512,512]{1,0:T(8,128)(2,1)} %copy-done.7) | copy-start | bytes 1572868
  270.6 2.6 copy-start.11
Sparse Core Ops, SparseCore 0:
  152.6 43.9 reduce-scatter.4
  199.3 49.1 reduce-scatter.2
